TPU v7x, 256 devices: a whole 4x4x8 slice. The times are simulated.
256 devices in a mesh: section: 8 (over x, core), dp: 32 (over y, z).
Axes of the slice: x: 4, y: 4, z: 8, core: 2. Of those that a mesh axis runs over, the one named last changes fastest.
Arguments:
- resid_in: bfloat16 [4, 1024, 2048], P(None, 'dp'), may hold values from -10 to 10
- dest_row: int32 [4, 1024], replicated, may hold values from 0 to 1023, as said below
- doc_ids: int32 [4, 1024], P(None, 'dp'), may hold values from 0 to 1023, as said below
- cotangent: bfloat16 [4, 1024, 2048], P(None, 'dp'), may hold values from -0.119628906 to 0.119628906
- gain: float32 [8, 2048], P('section'), may hold values from 0.5 to 1.5
- steer: float32 [8, 2048], P('section'), may hold values from -3 to 3
- w_query: bfloat16 [8, 2048, 1024], P('section', 'dp'), may hold values from -1 to 1
- w_keyval: bfloat16 [8, 2048, 512], P('section', 'dp'), may hold values from -1 to 1
- w_out: bfloat16 [8, 1024, 2048], P('section', None, 'dp'), may hold values from -0.1875 to 0.1875
Outputs:
- hidden_out: bfloat16 [8, 4, 1024, 2048], P('section', None, 'dp')
- grad_steer: float32 [8, 2048], P('section')
Inputs may be any that keep to these rules, and one draw needn't show every extreme that they name: Each row of dest_row is a permutation of 0 to 1023. Counting the tokens of one aligned block of 32 input tokens that go to one aligned block of 32 packed rows, no count exceeds 2, and some reach it in every micro-batch. doc_ids never falls along a row; every value is a row index r at which doc_ids equals r; each aligned block of 32 rows begins a document, so no document crosses such a block.
All inputs are finite; a program needn't handle non-finite values.
Results may differ from a plain program's by a relative error of at most 0.02.
Values may be sent and summed in bfloat16 or wider, within the bound.
No kernel may reach another device: no remote copies, remote signals or barrier semaphores. Data moves between devices by JAX's collectives and lax.ppermute only.
A program may use at most 64 MiB of HBM per device.

v0:
```python
import jax
import jax.numpy as jnp
from jax import lax
from jax.sharding import PartitionSpec as P

HD = 64
ROPE_BASE = 500000.0
EPSILON = 1e-05
MASKED = -1e30


def rotate(values, positions):
    half_size = values.shape[-1] // 2
    freq_index = jnp.arange(half_size, dtype=jnp.float32)
    inverse = ROPE_BASE ** (-2.0 * freq_index / values.shape[-1])
    angles = positions.astype(jnp.float32)[..., None] * inverse
    cosine = jnp.cos(angles)[..., None, :]
    sine_part = jnp.sin(angles)[..., None, :]
    first_half = values[..., :half_size]
    second = values[..., half_size:]
    return jnp.concatenate(
        [first_half * cosine - second * sine_part, second * cosine + first_half * sine_part],
        axis=-1,
    )


def layer(hidden_in, steering, gain_row, w_query, w_keyval, w_out, positions, documents):
    micro_count, row_count, width = hidden_in.shape
    head_size = HD
    kv_heads = w_keyval.shape[1] // (2 * head_size)
    query_heads = w_query.shape[1] // head_size
    group_size = query_heads // kv_heads
    residual = hidden_in.astype(jnp.float32) + steering
    normed = (
        residual
        * lax.rsqrt(jnp.mean(residual * residual, axis=-1, keepdims=True) + EPSILON)
        * gain_row
    ).astype(jnp.bfloat16)
    flat = normed.reshape(micro_count * row_count, width)
    queries = jnp.dot(flat, w_query, preferred_element_type=jnp.float32).reshape(
        micro_count, row_count, query_heads, head_size
    )
    keyval = jnp.dot(flat, w_keyval, preferred_element_type=jnp.float32).reshape(
        micro_count, row_count, 2 * kv_heads * head_size
    )
    key_rows = rotate(
        keyval[..., : kv_heads * head_size].reshape(micro_count, row_count, kv_heads, head_size),
        positions,
    ).astype(jnp.bfloat16)
    values = (
        keyval[..., kv_heads * head_size :]
        .reshape(micro_count, row_count, kv_heads, head_size)
        .astype(jnp.bfloat16)
    )
    queries = (
        rotate(queries, positions)
        .astype(jnp.bfloat16)
        .reshape(micro_count, row_count, kv_heads, group_size, head_size)
    )
    scores = jnp.einsum(
        "mrkgd,mskd->mkgrs", queries, key_rows, preferred_element_type=jnp.float32
    ) * head_size ** (-0.5)
    row_index = jnp.arange(row_count)
    allowed = (documents[:, :, None] == documents[:, None, :]) & (
        row_index[:, None] >= row_index[None, :]
    )
    scores = jnp.where(allowed[:, None, None], scores, MASKED)
    peak = jnp.max(scores, axis=-1, keepdims=True)
    weights = jnp.exp(scores - peak)
    weights = (weights / jnp.sum(weights, axis=-1, keepdims=True)).astype(jnp.bfloat16)
    mixed_heads = jnp.einsum(
        "mkgrs,mskd->mrkgd", weights, values, preferred_element_type=jnp.float32
    ).astype(jnp.bfloat16)
    mixed_heads = mixed_heads.reshape(micro_count * row_count, query_heads * head_size)
    projected = jnp.dot(mixed_heads, w_out, preferred_element_type=jnp.float32).reshape(
        micro_count, row_count, width
    )
    return (residual + projected).astype(jnp.bfloat16)


def plan_slots(target, device, row_count, capacity, dp_count):
    target_grid = target.reshape(dp_count, row_count)
    target_dev = target_grid // row_count
    target_off = target_grid % row_count
    row_order = jnp.arange(row_count, dtype=jnp.int32)
    matching = target_dev[:, :, None] == target_dev[:, None, :]
    earlier = row_order[None, :] < row_order[:, None]
    rank_ids = jnp.sum((matching & earlier[None]).astype(jnp.int32), axis=2)
    slot_ids = target_dev * capacity + rank_ids
    own_slot = lax.dynamic_index_in_dim(slot_ids, device, 0, keepdims=False)
    column_ids = jnp.arange(dp_count, dtype=jnp.int32)[:, None] * capacity + rank_ids
    landing = (target_dev == device)[None] & (target_off[None] == row_order[:, None, None])
    source_col = jnp.sum(jnp.where(landing, column_ids[None], 0), axis=(1, 2))
    return (own_slot, source_col)


def pack_rows(source_rows, own_slot, slot_count):
    selector = (jnp.arange(slot_count, dtype=jnp.int32)[:, None] == own_slot[None, :]).astype(
        jnp.bfloat16
    )
    return jnp.dot(selector, source_rows, preferred_element_type=jnp.float32).astype(jnp.bfloat16)


def unpack_rows(arrived, source_col):
    selector = (
        source_col[:, None] == jnp.arange(arrived.shape[0], dtype=jnp.int32)[None, :]
    ).astype(jnp.bfloat16)
    return jnp.dot(selector, arrived, preferred_element_type=jnp.float32).astype(jnp.bfloat16)


def body(resid_in, dest_row, doc_ids, cotangent, gain, steer, w_query, w_keyval, w_out):
    dp_count = lax.axis_size("dp")
    section_count = lax.axis_size("section")
    device = lax.axis_index("dp")
    section_idx = lax.axis_index("section")
    micro_count, row_count, width = resid_in.shape
    capacity = row_count // dp_count + 1
    slot_count = dp_count * capacity
    full_query, full_keyval, full_out = (
        lax.all_gather(w_query[0], "dp", axis=0, tiled=True),
        lax.all_gather(w_keyval[0], "dp", axis=0, tiled=True),
        lax.all_gather(w_out[0], "dp", axis=1, tiled=True),
    )
    gain_row = gain[0]
    steering = steer[0]
    plans = [
        plan_slots(dest_row[micro_idx], device, row_count, capacity, dp_count)
        for micro_idx in range(micro_count)
    ]
    packed = jnp.stack(
        [
            pack_rows(resid_in[micro_idx], plans[micro_idx][0], slot_count).reshape(
                dp_count, capacity, width
            )
            for micro_idx in range(micro_count)
        ],
        axis=1,
    )
    arrived = lax.all_to_all(packed, "dp", split_axis=0, concat_axis=0, tiled=True)
    grouped = jnp.stack(
        [
            unpack_rows(arrived[:, micro_idx].reshape(slot_count, width), plans[micro_idx][1])
            for micro_idx in range(micro_count)
        ]
    )
    global_rows = device * row_count + jnp.arange(row_count, dtype=jnp.int32)
    positions = global_rows[None, :] - doc_ids

    def run_layer(hidden_in, steer_vec):
        return layer(
            hidden_in, steer_vec, gain_row, full_query, full_keyval, full_out, positions, doc_ids
        )

    zero_block = jnp.zeros((micro_count, row_count, width), jnp.bfloat16)
    forward_route = [(i, i + 1) for i in range(section_count - 1)]
    backward_route = [(i + 1, i) for i in range(section_count - 1)]

    def forward_step(carry, step):
        incoming, kept, produced = carry
        active = section_idx == step
        hidden_in = jnp.where(step == 0, grouped, incoming)
        kept = jnp.where(active, hidden_in, kept)
        hidden_new = lax.cond(active, lambda: run_layer(hidden_in, steering), lambda: zero_block)
        produced = jnp.where(active, hidden_new, produced)
        sent = lax.ppermute(hidden_new, "section", forward_route)
        return ((sent, kept, produced), None)

    (unused_in, kept, produced), unused_ys = lax.scan(
        forward_step,
        (zero_block, zero_block, zero_block),
        jnp.arange(section_count, dtype=jnp.int32),
    )

    def backward_step(carry, step):
        incoming, grad_sum = carry
        active = section_idx == step
        upstream = jnp.where(step == section_count - 1, cotangent, incoming)

        def differentiate():
            unused_out, pullback = jax.vjp(run_layer, kept, steering)
            return pullback(upstream)

        grad_in, steer_part = lax.cond(
            active, differentiate, lambda: (zero_block, jnp.zeros_like(steering))
        )
        sent = lax.ppermute(grad_in, "section", backward_route)
        return ((sent, grad_sum + steer_part), None)

    (unused_grad, grad_sum), unused_zs = lax.scan(
        backward_step,
        (zero_block, jnp.zeros_like(steering)),
        jnp.arange(section_count - 1, -1, -1, dtype=jnp.int32),
    )
    total = lax.psum(grad_sum, "dp")
    return (produced[None], total[None])


def solution(mesh):
    in_specs = (
        P(None, "dp", None),
        P(),
        P(None, "dp"),
        P(None, "dp", None),
        P("section", None),
        P("section", None),
        P("section", "dp", None),
        P("section", "dp", None),
        P("section", None, "dp"),
    )
    out_specs = (P("section", None, "dp", None), P("section", None))
    return jax.shard_map(body, mesh=mesh, in_specs=in_specs, out_specs=out_specs, check_vma=False)
```

profile of v0, /device:TPU:0, one launch (start us, length us, event | category | flops | bytes accessed | tf_op | source)
XLA Modules:
  0.0 964.3 jit_solution(17783899758612930752)
XLA Ops:
  10.7 2.9 convert_reduce_fusion.4
  18.9 2.4 pad_maximum_fusion.3
  21.3 10.0 %all-to-all-start = ((bf16[32,4,2,2048]{3,2,1,0:T(2,128)(2,1)}), bf16[32,4,2,2048]{3,2,1,0:T(2,128)(2,1)S(1)}, u32[]{:S(2)}, u32[]{:S(2)}) async-start(bf16[32,4,2,2048]{3,2,1,0:T(2,128)(2,1)} %pad_maximum_fusion.3), calls=%async_computation | async-start | bytes 2097152 | tf_op jit(solution)/shard_map/all_to_all | solution.py:139
  36.0 26.9 %all-to-all-done = bf16[32,4,2,2048]{3,2,1,0:T(2,128)(2,1)S(1)} async-done(((bf16[32,4,2,2048]{3,2,1,0:T(2,128)(2,1)}), bf16[32,4,2,2048]{3,2,1,0:T(2,128)(2,1)S(1)}, u32[]{:S(2)}, u32[]{:S(2)}) %all-to-all-start) | async-done | bytes 1048608 | tf_op jit(solution)/shard_map/all_to_all | solution.py:139
  65.2 32.7 %all-gather.9.cloned.1.call-done = bf16[1,2048,1024]{2,1,0:T(8,128)(2,1)} async-done(((bf16[1,64,1024]{2,1,0:T(8,128)(2,1)}), bf16[1,2048,1024]{2,1,0:T(8,128)(2,1)}) %all-gather.9.cloned.1.call-update) | async-done | bytes 4194320 | tf_op jit(solution)/shard_map/all_gather | solution.py:120
  97.9 6.5 copy.79
  104.4 74.7 %all-gather.11.cloned.1.call-done = bf16[1,1024,2048]{1,2,0:T(8,128)(2,1)} async-done(((bf16[1,1024,64]{1,2,0:T(8,128)(2,1)}), bf16[1,1024,2048]{1,2,0:T(8,128)(2,1)}) %all-gather.11.cloned.1.call-update) | async-done | bytes 4194320 | tf_op jit(solution)/shard_map/all_gather | solution.py:122
  179.1 6.5 copy.80
  185.6 71.0 %all-gather.7.cloned.1.call-done = bf16[1,2048,512]{2,1,0:T(8,128)(2,1)} async-done(((bf16[1,64,512]{2,1,0:T(8,128)(2,1)}), bf16[1,2048,512]{2,1,0:T(8,128)(2,1)}) %all-gather.7.cloned.1.call-update) | async-done | bytes 2097168 | tf_op jit(solution)/shard_map/all_gather | solution.py:121
  256.7 157.6 %while.28 = (s32[]{:T(128)}, bf16[4,32,2048]{2,1,0:T(8,128)(2,1)S(1)}, bf16[4,32,2048]{2,1,0:T(8,128)(2,1)S(1)}, bf16[4,32,2048]{2,1,0:T(8,128)(2,1)}, s32[8]{0:...) while((s32[]{:T(128)}, ...), condition=%wide.region_14.15_spmd.clone, body=%wide.region_8.14_spmd.clone.sunk | while | flops 1376075008 | bytes 24693816 | solution.py:168
  258.7 18.0 %conditional.6 = (bf16[4,32,2048]{2,1,0:T(8,128)(2,1)S(1)}) conditional(s32[]{:T(128)} %convert_element_type.335, () %tuple.113, (bf16[4,32,2048]{2,1,0:T(8,128)(2,1)S(1)}, f32[1,2048]{1,0:T(1,128)}, f32[1,2048]{1,0:T(1,128)}, bf16[2048,512]{1,0:T(8,128)(2,1)}, s32[4,32]{1,0:T(4,128)}, /*index=5*/s32[4,32]{1,0:T(4,128)}, ...), branch_computations={%region_9.9_spmd, %region_10.13_spmd} | conditional | flops 1374764288 | bytes 18402056 | solution.py:163
  259.6 2.1 fusion.9
  263.2 4.5 fusion.19
  270.9 2.2 fusion.15
  273.7 2.9 fusion.6
  281.5 20.2 %collective-permute-start = (bf16[4,32,2048]{2,1,0:T(8,128)(2,1)S(1)}, bf16[4,32,2048]{2,1,0:T(8,128)(2,1)S(1)}, u32[]{:S(2)}, u32[]{:S(2)}) collective-permute-start(bf16[4,32,2048]{2,1,0:T(8,128)(2,1)S(1)} %get-tuple-element.784), channel_id=1, source_target_pairs={{0,32},{32,64},{64,96},{96,128},{128,160},{160,192},{192,224},{1,3... | collective-permute-start | bytes 1572872 | tf_op jit(solution)/shard_map/while/body/eval_jaxpr/ppermute | solution.py:165
  301.7 1.9 select_select_fusion.5
  305.7 6.1 collective-permute-start
  311.8 1.9 select_select_fusion.5
  315.8 26.5 %collective-permute-start = (bf16[4,32,2048]{2,1,0:T(8,128)(2,1)S(1)}, bf16[4,32,2048]{2,1,0:T(8,128)(2,1)S(1)}, u32[]{:S(2)}, u32[]{:S(2)}) collective-permute-start(bf16[4,32,2048]{2,1,0:T(8,128)(2,1)S(1)} %get-tuple-element.784), channel_id=1, source_target_pairs={{0,32},{32,64},{64,96},{96,128},{128,160},{160,192},{192,224},{1,3... | collective-permute-start | bytes 1572872 | tf_op jit(solution)/shard_map/while/body/eval_jaxpr/ppermute | solution.py:165
  342.2 1.9 select_select_fusion.5
  346.2 8.6 collective-permute-start
  354.8 1.9 select_select_fusion.5
  358.7 13.1 %collective-permute-start = (bf16[4,32,2048]{2,1,0:T(8,128)(2,1)S(1)}, bf16[4,32,2048]{2,1,0:T(8,128)(2,1)S(1)}, u32[]{:S(2)}, u32[]{:S(2)}) collective-permute-start(bf16[4,32,2048]{2,1,0:T(8,128)(2,1)S(1)} %get-tuple-element.784), channel_id=1, source_target_pairs={{0,32},{32,64},{64,96},{96,128},{128,160},{160,192},{192,224},{1,3... | collective-permute-start | bytes 1572872 | tf_op jit(solution)/shard_map/while/body/eval_jaxpr/ppermute | solution.py:165
  371.8 1.9 select_select_fusion.5
  375.8 8.6 collective-permute-start
  384.4 1.9 select_select_fusion.5
  388.3 24.0 %collective-permute-start = (bf16[4,32,2048]{2,1,0:T(8,128)(2,1)S(1)}, bf16[4,32,2048]{2,1,0:T(8,128)(2,1)S(1)}, u32[]{:S(2)}, u32[]{:S(2)}) collective-permute-start(bf16[4,32,2048]{2,1,0:T(8,128)(2,1)S(1)} %get-tuple-element.784), channel_id=1, source_target_pairs={{0,32},{32,64},{64,96},{96,128},{128,160},{160,192},{192,224},{1,3... | collective-permute-start | bytes 1572872 | tf_op jit(solution)/shard_map/while/body/eval_jaxpr/ppermute | solution.py:165
  412.3 1.9 select_select_fusion.5
  415.2 469.1 %while.29 = (s32[]{:T(128)}, bf16[4,32,2048]{2,1,0:T(8,128)(2,1)}, f32[2048]{0:T(1024)}, s32[8]{0:T(128)}, s32[]{:T(128)}, /*index=5*/bf16[4,32,2048]{2,1,0:T(8,...) while((s32[]{:T(128)}, bf16[4,32,2048]{2,1,0:T(8,128)(2,1)}, ...), condition=%wide.region_26.27_spmd.clone, body=%wide.region_15.26_spmd.clone.sunk | while | flops 2205098752 | bytes 54051516 | solution.py:189
  417.2 1.5 conditional.7
  421.3 7.6 collective-permute-done.1
  435.8 13.3 %collective-permute-done.1 = bf16[4,32,2048]{2,1,0:T(8,128)(2,1)S(1)} collective-permute-done((bf16[4,32,2048]{2,1,0:T(8,128)(2,1)}, bf16[4,32,2048]{2,1,0:T(8,128)(2,1)S(1)}, u32[]{:S(2)}, u32[]{:S(2)}) %collective-permute-start.1) | collective-permute-done | bytes 524320 | tf_op jit(solution)/shard_map/while/body/eval_jaxpr/ppermute | solution.py:186
  456.2 8.1 collective-permute-done.1
  471.2 23.7 %collective-permute-done.1 = bf16[4,32,2048]{2,1,0:T(8,128)(2,1)S(1)} collective-permute-done((bf16[4,32,2048]{2,1,0:T(8,128)(2,1)}, bf16[4,32,2048]{2,1,0:T(8,128)(2,1)S(1)}, u32[]{:S(2)}, u32[]{:S(2)}) %collective-permute-start.1) | collective-permute-done | bytes 524320 | tf_op jit(solution)/shard_map/while/body/eval_jaxpr/ppermute | solution.py:186
  502.0 8.1 collective-permute-done.1
  517.0 12.8 %collective-permute-done.1 = bf16[4,32,2048]{2,1,0:T(8,128)(2,1)S(1)} collective-permute-done((bf16[4,32,2048]{2,1,0:T(8,128)(2,1)}, bf16[4,32,2048]{2,1,0:T(8,128)(2,1)S(1)}, u32[]{:S(2)}, u32[]{:S(2)}) %collective-permute-start.1) | collective-permute-done | bytes 524320 | tf_op jit(solution)/shard_map/while/body/eval_jaxpr/ppermute | solution.py:186
  536.9 295.9 %collective-permute-done.1 = bf16[4,32,2048]{2,1,0:T(8,128)(2,1)S(1)} collective-permute-done((bf16[4,32,2048]{2,1,0:T(8,128)(2,1)}, bf16[4,32,2048]{2,1,0:T(8,128)(2,1)S(1)}, u32[]{:S(2)}, u32[]{:S(2)}) %collective-permute-start.1) | collective-permute-done | bytes 524320 | tf_op jit(solution)/shard_map/while/body/eval_jaxpr/ppermute | solution.py:186
  835.7 43.7 %conditional.7 = (bf16[4,32,2048]{2,1,0:T(8,128)(2,1)}, f32[2048]{0:T(1024)}) conditional(s32[]{:T(128)} %convert_element_type.336, () %tuple.116, (s32[]{:T(128)}, bf16[4,32,2048]{2,1,0:T(8,128)(2,1)}, bf16[4,32,2048]{2,1,0:T(8,128)(2,1)}, bf16[1024,2048]{1,0:T(8,128)(2,1)}, s32[4,32]{1,0:T(4,128)}, ...), branch_computations={%region_16.16_spmd, %region_17.25_spmd} | conditional | flops 2205094656 | bytes 49832296 | solution.py:183
  837.1 2.1 fusion.47
  841.5 4.6 fusion.71
  851.8 3.7 convolution_convert_fusion.5
  856.7 1.5 fusion.54
  860.8 2.0 fusion.62
  866.9 1.8 fusion.49
  872.0 2.9 fusion.139
  876.8 2.6 fusion.78
  884.3 73.4 %psum.7 = f32[1,2048]{1,0:T(1,128)} all-reduce(f32[1,2048]{1,0:T(1,128)} %bitcast.243), channel_id=1, replica_groups=mesh['section'=8,'dp'=32] {'dp'}, use_global_device_ids=true, to_apply=%region_27.28 | all-reduce | flops 2048 | bytes 16384 | tf_op jit(solution)/shard_map/psum | solution.py:194
  (253 shorter events, 113.5 us)
Async XLA Ops:
  7.2 90.8 %all-gather.9.cloned.1.call-start = ((), (), s32[]{:S(2)}) async-start(), calls=%async_computation.2 | async-start | bytes 4325376 | tf_op jit(solution)/shard_map/all_gather | solution.py:120
  7.9 171.2 %all-gather.11.cloned.1.call-start = ((), (), s32[]{:S(2)}) async-start(), calls=%async_computation.3 | async-start | bytes 4325376 | tf_op jit(solution)/shard_map/all_gather | solution.py:122
  8.6 248.0 %all-gather.7.cloned.1.call-start = ((), (), s32[]{:S(2)}) async-start(), calls=%async_computation.1 | async-start | bytes 2162688 | tf_op jit(solution)/shard_map/all_gather | solution.py:121
  21.3 41.6 %all-to-all-start = ((bf16[32,4,2,2048]{3,2,1,0:T(2,128)(2,1)}), bf16[32,4,2,2048]{3,2,1,0:T(2,128)(2,1)S(1)}, u32[]{:S(2)}, u32[]{:S(2)}) async-start(bf16[32,4,2,2048]{3,2,1,0:T(2,128)(2,1)} %pad_maximum_fusion.3), calls=%async_computation | async-start | bytes 2097152 | tf_op jit(solution)/shard_map/all_to_all | solution.py:139
  276.6 2.8 collective-permute-start
  281.5 22.1 %collective-permute-start = (bf16[4,32,2048]{2,1,0:T(8,128)(2,1)S(1)}, bf16[4,32,2048]{2,1,0:T(8,128)(2,1)S(1)}, u32[]{:S(2)}, u32[]{:S(2)}) collective-permute-start(bf16[4,32,2048]{2,1,0:T(8,128)(2,1)S(1)} %get-tuple-element.784), channel_id=1, source_target_pairs={{0,32},{32,64},{64,96},{96,128},{128,160},{160,192},{192,224},{1,3... | collective-permute-start | bytes 1572872 | tf_op jit(solution)/shard_map/while/body/eval_jaxpr/ppermute | solution.py:165
  305.7 8.0 collective-permute-start
  315.8 28.4 %collective-permute-start = (bf16[4,32,2048]{2,1,0:T(8,128)(2,1)S(1)}, bf16[4,32,2048]{2,1,0:T(8,128)(2,1)S(1)}, u32[]{:S(2)}, u32[]{:S(2)}) collective-permute-start(bf16[4,32,2048]{2,1,0:T(8,128)(2,1)S(1)} %get-tuple-element.784), channel_id=1, source_target_pairs={{0,32},{32,64},{64,96},{96,128},{128,160},{160,192},{192,224},{1,3... | collective-permute-start | bytes 1572872 | tf_op jit(solution)/shard_map/while/body/eval_jaxpr/ppermute | solution.py:165
  346.2 10.5 %collective-permute-start = (bf16[4,32,2048]{2,1,0:T(8,128)(2,1)S(1)}, bf16[4,32,2048]{2,1,0:T(8,128)(2,1)S(1)}, u32[]{:S(2)}, u32[]{:S(2)}) collective-permute-start(bf16[4,32,2048]{2,1,0:T(8,128)(2,1)S(1)} %get-tuple-element.784), channel_id=1, source_target_pairs={{0,32},{32,64},{64,96},{96,128},{128,160},{160,192},{192,224},{1,3... | collective-permute-start | bytes 1572872 | tf_op jit(solution)/shard_map/while/body/eval_jaxpr/ppermute | solution.py:165
  358.7 15.0 %collective-permute-start = (bf16[4,32,2048]{2,1,0:T(8,128)(2,1)S(1)}, bf16[4,32,2048]{2,1,0:T(8,128)(2,1)S(1)}, u32[]{:S(2)}, u32[]{:S(2)}) collective-permute-start(bf16[4,32,2048]{2,1,0:T(8,128)(2,1)S(1)} %get-tuple-element.784), channel_id=1, source_target_pairs={{0,32},{32,64},{64,96},{96,128},{128,160},{160,192},{192,224},{1,3... | collective-permute-start | bytes 1572872 | tf_op jit(solution)/shard_map/while/body/eval_jaxpr/ppermute | solution.py:165
  375.8 10.5 %collective-permute-start = (bf16[4,32,2048]{2,1,0:T(8,128)(2,1)S(1)}, bf16[4,32,2048]{2,1,0:T(8,128)(2,1)S(1)}, u32[]{:S(2)}, u32[]{:S(2)}) collective-permute-start(bf16[4,32,2048]{2,1,0:T(8,128)(2,1)S(1)} %get-tuple-element.784), channel_id=1, source_target_pairs={{0,32},{32,64},{64,96},{96,128},{128,160},{160,192},{192,224},{1,3... | collective-permute-start | bytes 1572872 | tf_op jit(solution)/shard_map/while/body/eval_jaxpr/ppermute | solution.py:165
  388.3 25.9 %collective-permute-start = (bf16[4,32,2048]{2,1,0:T(8,128)(2,1)S(1)}, bf16[4,32,2048]{2,1,0:T(8,128)(2,1)S(1)}, u32[]{:S(2)}, u32[]{:S(2)}) collective-permute-start(bf16[4,32,2048]{2,1,0:T(8,128)(2,1)S(1)} %get-tuple-element.784), channel_id=1, source_target_pairs={{0,32},{32,64},{64,96},{96,128},{128,160},{160,192},{192,224},{1,3... | collective-permute-start | bytes 1572872 | tf_op jit(solution)/shard_map/while/body/eval_jaxpr/ppermute | solution.py:165
  418.7 10.2 %collective-permute-start.1 = (bf16[4,32,2048]{2,1,0:T(8,128)(2,1)}, bf16[4,32,2048]{2,1,0:T(8,128)(2,1)S(1)}, u32[]{:S(2)}, u32[]{:S(2)}) collective-permute-start(bf16[4,32,2048]{2,1,0:T(8,128)(2,1)} %get-tuple-element.682), channel_id=1, source_target_pairs={{32,0},{64,32},{96,64},{128,96},{160,128},{192,160},{224,192},{33,... | collective-permute-start | bytes 1572872 | tf_op jit(solution)/shard_map/while/body/eval_jaxpr/ppermute | solution.py:186
  428.8 0.9 copy-start.1
  433.2 15.9 %collective-permute-start.1 = (bf16[4,32,2048]{2,1,0:T(8,128)(2,1)}, bf16[4,32,2048]{2,1,0:T(8,128)(2,1)S(1)}, u32[]{:S(2)}, u32[]{:S(2)}) collective-permute-start(bf16[4,32,2048]{2,1,0:T(8,128)(2,1)} %get-tuple-element.682), channel_id=1, source_target_pairs={{32,0},{64,32},{96,64},{128,96},{160,128},{192,160},{224,192},{33,... | collective-permute-start | bytes 1572872 | tf_op jit(solution)/shard_map/while/body/eval_jaxpr/ppermute | solution.py:186
  449.2 0.9 copy-start.1
  453.6 10.7 %collective-permute-start.1 = (bf16[4,32,2048]{2,1,0:T(8,128)(2,1)}, bf16[4,32,2048]{2,1,0:T(8,128)(2,1)S(1)}, u32[]{:S(2)}, u32[]{:S(2)}) collective-permute-start(bf16[4,32,2048]{2,1,0:T(8,128)(2,1)} %get-tuple-element.682), channel_id=1, source_target_pairs={{32,0},{64,32},{96,64},{128,96},{160,128},{192,160},{224,192},{33,... | collective-permute-start | bytes 1572872 | tf_op jit(solution)/shard_map/while/body/eval_jaxpr/ppermute | solution.py:186
  464.2 0.9 copy-start.1
  468.6 26.3 %collective-permute-start.1 = (bf16[4,32,2048]{2,1,0:T(8,128)(2,1)}, bf16[4,32,2048]{2,1,0:T(8,128)(2,1)S(1)}, u32[]{:S(2)}, u32[]{:S(2)}) collective-permute-start(bf16[4,32,2048]{2,1,0:T(8,128)(2,1)} %get-tuple-element.682), channel_id=1, source_target_pairs={{32,0},{64,32},{96,64},{128,96},{160,128},{192,160},{224,192},{33,... | collective-permute-start | bytes 1572872 | tf_op jit(solution)/shard_map/while/body/eval_jaxpr/ppermute | solution.py:186
  495.0 0.9 copy-start.1
  499.3 10.7 %collective-permute-start.1 = (bf16[4,32,2048]{2,1,0:T(8,128)(2,1)}, bf16[4,32,2048]{2,1,0:T(8,128)(2,1)S(1)}, u32[]{:S(2)}, u32[]{:S(2)}) collective-permute-start(bf16[4,32,2048]{2,1,0:T(8,128)(2,1)} %get-tuple-element.682), channel_id=1, source_target_pairs={{32,0},{64,32},{96,64},{128,96},{160,128},{192,160},{224,192},{33,... | collective-permute-start | bytes 1572872 | tf_op jit(solution)/shard_map/while/body/eval_jaxpr/ppermute | solution.py:186
  510.0 0.9 copy-start.1
  514.4 15.4 %collective-permute-start.1 = (bf16[4,32,2048]{2,1,0:T(8,128)(2,1)}, bf16[4,32,2048]{2,1,0:T(8,128)(2,1)S(1)}, u32[]{:S(2)}, u32[]{:S(2)}) collective-permute-start(bf16[4,32,2048]{2,1,0:T(8,128)(2,1)} %get-tuple-element.682), channel_id=1, source_target_pairs={{32,0},{64,32},{96,64},{128,96},{160,128},{192,160},{224,192},{33,... | collective-permute-start | bytes 1572872 | tf_op jit(solution)/shard_map/while/body/eval_jaxpr/ppermute | solution.py:186
  529.9 0.9 copy-start.1
  534.2 298.5 %collective-permute-start.1 = (bf16[4,32,2048]{2,1,0:T(8,128)(2,1)}, bf16[4,32,2048]{2,1,0:T(8,128)(2,1)S(1)}, u32[]{:S(2)}, u32[]{:S(2)}) collective-permute-start(bf16[4,32,2048]{2,1,0:T(8,128)(2,1)} %get-tuple-element.682), channel_id=1, source_target_pairs={{32,0},{64,32},{96,64},{128,96},{160,128},{192,160},{224,192},{33,... | collective-permute-start | bytes 1572872 | tf_op jit(solution)/shard_map/while/body/eval_jaxpr/ppermute | solution.py:186
  832.8 0.9 copy-start.1
  836.6 4.8 copy-start.20
  839.3 0.7 copy-start.13
  841.4 6.6 copy-start.2
  841.4 6.6 copy-start.4
  849.1 1.6 copy-start.8
  856.7 2.4 copy-start.11
  856.7 4.0 copy-start.9
  860.7 3.0 copy-start.10
  860.7 3.0 copy-start.12
  860.8 3.0 copy-start.18
  862.8 1.9 copy-start.7
  862.8 1.8 copy-start.14
  863.7 1.2 copy-start.15
  863.7 3.2 copy-start.3
  863.7 3.1 copy-start.5
  863.7 3.1 copy-start.19
  869.1 5.8 copy-start
  869.1 5.8 copy-start.6
  872.0 4.8 copy-start.17
  872.0 4.8 copy-start.21
  879.4 4.0 collective-permute-start.1
  883.4 0.9 copy-start.1
  (1 other events, 0.5 us)
Sparse Core Ops, SparseCore 0:
  10.6 87.3 all-gather.8
  100.5 78.5 all-gather.10
  181.7 74.8 all-gather.6
where the time goes:
time: 967 us; the launch traced here: 964 us
  waiting for transfers between devices  579 us (60%)
  starting transfers between devices  129 us (13%)
  blocking collectives  73.4 us (8%)
  local copies, waits for them, and re-layouts  59.4 us (6%)
  other arithmetic  54 us (6%)
  matrix products  39.5 us (4%)
  loops' own time  16.4 us (2%)
  between operations  14 us (1%)
    ppermute x8, waiting for transfers between devices, backward_step(): sent = lax.ppermute(grad_in, 'section', backward_route)  371 us
    ppermute x8, starting transfers between devices, forward_step(): sent = lax.ppermute(hidden_new, 'section', forward_route)  108 us
    all_gather x1, waiting for transfers between devices, body(): lax.all_gather(w_out[0], 'dp', axis=1, tiled=True)  74.7 us
    psum x1, blocking collectives, body(): total = lax.psum(grad_sum, 'dp')  73.4 us
    all_gather x1, waiting for transfers between devices, body(): lax.all_gather(w_keyval[0], 'dp', axis=0, tiled=True)  71 us
    all_gather x1, waiting for transfers between devices, body(): lax.all_gather(w_query[0], 'dp', axis=0, tiled=True)  32.7 us
    all_to_all x1, waiting for transfers between devices, body(): lax.all_to_all(packed, 'dp', split_axis=0, concat_axis=0, tiled=True)  26.9 us
  transfers between devices with their start and end apart: 20, of which 13 were waited for; matrix products, arithmetic and copies ran while one was open for 6% of the time, Pallas kernels for 0%

commit v1 on v0

--- a/solution.py
+++ b/solution.py
@@ -1,3 +1,4 @@
+import functools
 import jax
 import jax.numpy as jnp
 from jax import lax
@@ -7,6 +8,15 @@
 ROPE_BASE = 500000.0
 EPSILON = 1e-05
 MASKED = -1e30
+
+
+def treat_view_on_mesh(packet, group_axis):
+    outcome_arr = lax.all_gather(packet, group_axis)
+    x_new = jnp.sum(outcome_arr, axis=0)
+    return x_new
+
+
+unite_roads_over_axis = functools.partial(treat_view_on_mesh, group_axis="dp")
 
 
 def rotate(values, positions):
@@ -191,7 +201,7 @@
         (zero_block, jnp.zeros_like(steering)),
         jnp.arange(section_count - 1, -1, -1, dtype=jnp.int32),
     )
-    total = lax.psum(grad_sum, "dp")
+    total = unite_roads_over_axis(grad_sum)
     return (produced[None], total[None])
 
 

time: 967 us -> 942 us (0.974)
  blocking collectives: 73.4 us -> 47.8 us
    psum x1 -> x0, blocking collectives: 73.4 us -> none  [body(): total = lax.psum(grad_sum, 'dp')]
    all_gather x0 -> x1, blocking collectives: none -> 47.8 us  [treat_view_on_mesh(): outcome_arr = lax.all_gather(packet, group_axis)]
where the time goes in v1:
time: 942 us; the launch traced here: 939 us
  waiting for transfers between devices  579 us (61%)
  starting transfers between devices  129 us (14%)
  local copies, waits for them, and re-layouts  59.4 us (6%)
  other arithmetic  54.6 us (6%)
  blocking collectives  47.8 us (5%)
  matrix products  39.5 us (4%)
  loops' own time  16.4 us (2%)
  between operations  14 us (1%)
    ppermute x8, waiting for transfers between devices, backward_step(): sent = lax.ppermute(grad_in, 'section', backward_route)  371 us
    ppermute x8, starting transfers between devices, forward_step(): sent = lax.ppermute(hidden_new, 'section', forward_route)  108 us
    all_gather x1, waiting for transfers between devices, body(): lax.all_gather(w_out[0], 'dp', axis=1, tiled=True)  74.7 us
    all_gather x1, waiting for transfers between devices, body(): lax.all_gather(w_keyval[0], 'dp', axis=0, tiled=True)  71 us
    all_gather x1, blocking collectives, treat_view_on_mesh(): outcome_arr = lax.all_gather(packet, group_axis)  47.8 us
    all_gather x1, waiting for transfers between devices, body(): lax.all_gather(w_query[0], 'dp', axis=0, tiled=True)  32.7 us
    all_to_all x1, waiting for transfers between devices, body(): lax.all_to_all(packed, 'dp', split_axis=0, concat_axis=0, tiled=True)  26.9 us
  transfers between devices with their start and end apart: 20, of which 13 were waited for; matrix products, arithmetic and copies ran while one was open for 6% of the time, Pallas kernels for 0%

profile of v1, /device:TPU:0, one launch (start us, length us, event | category | flops | bytes accessed | tf_op | source)
XLA Modules:
  0.0 939.2 jit_solution(15473372592379680056)
XLA Ops:
  10.7 2.9 convert_reduce_fusion.4
  18.9 2.4 pad_maximum_fusion.3
  21.3 10.0 %all-to-all-start = ((bf16[32,4,2,2048]{3,2,1,0:T(2,128)(2,1)}), bf16[32,4,2,2048]{3,2,1,0:T(2,128)(2,1)S(1)}, u32[]{:S(2)}, u32[]{:S(2)}) async-start(bf16[32,4,2,2048]{3,2,1,0:T(2,128)(2,1)} %pad_maximum_fusion.3), calls=%async_computation | async-start | bytes 2097152 | tf_op jit(solution)/shard_map/all_to_all | solution.py:149
  36.0 26.9 %all-to-all-done = bf16[32,4,2,2048]{3,2,1,0:T(2,128)(2,1)S(1)} async-done(((bf16[32,4,2,2048]{3,2,1,0:T(2,128)(2,1)}), bf16[32,4,2,2048]{3,2,1,0:T(2,128)(2,1)S(1)}, u32[]{:S(2)}, u32[]{:S(2)}) %all-to-all-start) | async-done | bytes 1048608 | tf_op jit(solution)/shard_map/all_to_all | solution.py:149
  65.2 32.7 %all-gather.10.cloned.1.call-done = bf16[1,2048,1024]{2,1,0:T(8,128)(2,1)} async-done(((bf16[1,64,1024]{2,1,0:T(8,128)(2,1)}), bf16[1,2048,1024]{2,1,0:T(8,128)(2,1)}) %all-gather.10.cloned.1.call-update) | async-done | bytes 4194320 | tf_op jit(solution)/shard_map/all_gather | solution.py:130
  97.9 6.5 copy.79
  104.4 74.7 %all-gather.12.cloned.1.call-done = bf16[1,1024,2048]{1,2,0:T(8,128)(2,1)} async-done(((bf16[1,1024,64]{1,2,0:T(8,128)(2,1)}), bf16[1,1024,2048]{1,2,0:T(8,128)(2,1)}) %all-gather.12.cloned.1.call-update) | async-done | bytes 4194320 | tf_op jit(solution)/shard_map/all_gather | solution.py:132
  179.1 6.5 copy.80
  185.6 71.0 %all-gather.8.cloned.1.call-done = bf16[1,2048,512]{2,1,0:T(8,128)(2,1)} async-done(((bf16[1,64,512]{2,1,0:T(8,128)(2,1)}), bf16[1,2048,512]{2,1,0:T(8,128)(2,1)}) %all-gather.8.cloned.1.call-update) | async-done | bytes 2097168 | tf_op jit(solution)/shard_map/all_gather | solution.py:131
  256.7 157.6 %while.28 = (s32[]{:T(128)}, bf16[4,32,2048]{2,1,0:T(8,128)(2,1)S(1)}, bf16[4,32,2048]{2,1,0:T(8,128)(2,1)S(1)}, bf16[4,32,2048]{2,1,0:T(8,128)(2,1)}, s32[8]{0:...) while((s32[]{:T(128)}, ...), condition=%wide.region_14.15_spmd.clone, body=%wide.region_8.14_spmd.clone.sunk | while | flops 1376075008 | bytes 24693816 | solution.py:178
  258.7 18.0 %conditional.6 = (bf16[4,32,2048]{2,1,0:T(8,128)(2,1)S(1)}) conditional(s32[]{:T(128)} %convert_element_type.335, () %tuple.113, (bf16[4,32,2048]{2,1,0:T(8,128)(2,1)S(1)}, f32[1,2048]{1,0:T(1,128)}, f32[1,2048]{1,0:T(1,128)}, bf16[2048,512]{1,0:T(8,128)(2,1)}, s32[4,32]{1,0:T(4,128)}, /*index=5*/s32[4,32]{1,0:T(4,128)}, ...), branch_computations={%region_9.9_spmd, %region_10.13_spmd} | conditional | flops 1374764288 | bytes 18402056 | solution.py:173
  259.6 2.1 fusion.9
  263.2 4.5 fusion.19
  270.9 2.2 fusion.15
  273.7 2.9 fusion.6
  281.5 20.2 %collective-permute-start = (bf16[4,32,2048]{2,1,0:T(8,128)(2,1)S(1)}, bf16[4,32,2048]{2,1,0:T(8,128)(2,1)S(1)}, u32[]{:S(2)}, u32[]{:S(2)}) collective-permute-start(bf16[4,32,2048]{2,1,0:T(8,128)(2,1)S(1)} %get-tuple-element.784), channel_id=1, source_target_pairs={{0,32},{32,64},{64,96},{96,128},{128,160},{160,192},{192,224},{1,3... | collective-permute-start | bytes 1572872 | tf_op jit(solution)/shard_map/while/body/eval_jaxpr/ppermute | solution.py:175
  301.7 1.9 select_select_fusion.5
  305.7 6.1 collective-permute-start
  311.8 1.9 select_select_fusion.5
  315.8 26.5 %collective-permute-start = (bf16[4,32,2048]{2,1,0:T(8,128)(2,1)S(1)}, bf16[4,32,2048]{2,1,0:T(8,128)(2,1)S(1)}, u32[]{:S(2)}, u32[]{:S(2)}) collective-permute-start(bf16[4,32,2048]{2,1,0:T(8,128)(2,1)S(1)} %get-tuple-element.784), channel_id=1, source_target_pairs={{0,32},{32,64},{64,96},{96,128},{128,160},{160,192},{192,224},{1,3... | collective-permute-start | bytes 1572872 | tf_op jit(solution)/shard_map/while/body/eval_jaxpr/ppermute | solution.py:175
  342.2 1.9 select_select_fusion.5
  346.2 8.6 collective-permute-start
  354.8 1.9 select_select_fusion.5
  358.7 13.1 %collective-permute-start = (bf16[4,32,2048]{2,1,0:T(8,128)(2,1)S(1)}, bf16[4,32,2048]{2,1,0:T(8,128)(2,1)S(1)}, u32[]{:S(2)}, u32[]{:S(2)}) collective-permute-start(bf16[4,32,2048]{2,1,0:T(8,128)(2,1)S(1)} %get-tuple-element.784), channel_id=1, source_target_pairs={{0,32},{32,64},{64,96},{96,128},{128,160},{160,192},{192,224},{1,3... | collective-permute-start | bytes 1572872 | tf_op jit(solution)/shard_map/while/body/eval_jaxpr/ppermute | solution.py:175
  371.8 1.9 select_select_fusion.5
  375.8 8.6 collective-permute-start
  384.4 1.9 select_select_fusion.5
  388.3 24.0 %collective-permute-start = (bf16[4,32,2048]{2,1,0:T(8,128)(2,1)S(1)}, bf16[4,32,2048]{2,1,0:T(8,128)(2,1)S(1)}, u32[]{:S(2)}, u32[]{:S(2)}) collective-permute-start(bf16[4,32,2048]{2,1,0:T(8,128)(2,1)S(1)} %get-tuple-element.784), channel_id=1, source_target_pairs={{0,32},{32,64},{64,96},{96,128},{128,160},{160,192},{192,224},{1,3... | collective-permute-start | bytes 1572872 | tf_op jit(solution)/shard_map/while/body/eval_jaxpr/ppermute | solution.py:175
  412.3 1.9 select_select_fusion.5
  415.2 469.1 %while.29 = (s32[]{:T(128)}, bf16[4,32,2048]{2,1,0:T(8,128)(2,1)}, f32[2048]{0:T(1024)}, s32[8]{0:T(128)}, s32[]{:T(128)}, /*index=5*/bf16[4,32,2048]{2,1,0:T(8,...) while((s32[]{:T(128)}, bf16[4,32,2048]{2,1,0:T(8,128)(2,1)}, ...), condition=%wide.region_26.27_spmd.clone, body=%wide.region_15.26_spmd.clone.sunk | while | flops 2205098752 | bytes 54051516 | solution.py:199
  417.2 1.5 conditional.7
  421.3 7.6 collective-permute-done.1
  435.8 13.3 %collective-permute-done.1 = bf16[4,32,2048]{2,1,0:T(8,128)(2,1)S(1)} collective-permute-done((bf16[4,32,2048]{2,1,0:T(8,128)(2,1)}, bf16[4,32,2048]{2,1,0:T(8,128)(2,1)S(1)}, u32[]{:S(2)}, u32[]{:S(2)}) %collective-permute-start.1) | collective-permute-done | bytes 524320 | tf_op jit(solution)/shard_map/while/body/eval_jaxpr/ppermute | solution.py:196
  456.2 8.1 collective-permute-done.1
  471.2 23.7 %collective-permute-done.1 = bf16[4,32,2048]{2,1,0:T(8,128)(2,1)S(1)} collective-permute-done((bf16[4,32,2048]{2,1,0:T(8,128)(2,1)}, bf16[4,32,2048]{2,1,0:T(8,128)(2,1)S(1)}, u32[]{:S(2)}, u32[]{:S(2)}) %collective-permute-start.1) | collective-permute-done | bytes 524320 | tf_op jit(solution)/shard_map/while/body/eval_jaxpr/ppermute | solution.py:196
  502.0 8.1 collective-permute-done.1
  517.0 12.8 %collective-permute-done.1 = bf16[4,32,2048]{2,1,0:T(8,128)(2,1)S(1)} collective-permute-done((bf16[4,32,2048]{2,1,0:T(8,128)(2,1)}, bf16[4,32,2048]{2,1,0:T(8,128)(2,1)S(1)}, u32[]{:S(2)}, u32[]{:S(2)}) %collective-permute-start.1) | collective-permute-done | bytes 524320 | tf_op jit(solution)/shard_map/while/body/eval_jaxpr/ppermute | solution.py:196
  536.9 295.9 %collective-permute-done.1 = bf16[4,32,2048]{2,1,0:T(8,128)(2,1)S(1)} collective-permute-done((bf16[4,32,2048]{2,1,0:T(8,128)(2,1)}, bf16[4,32,2048]{2,1,0:T(8,128)(2,1)S(1)}, u32[]{:S(2)}, u32[]{:S(2)}) %collective-permute-start.1) | collective-permute-done | bytes 524320 | tf_op jit(solution)/shard_map/while/body/eval_jaxpr/ppermute | solution.py:196
  835.7 43.7 %conditional.7 = (bf16[4,32,2048]{2,1,0:T(8,128)(2,1)}, f32[2048]{0:T(1024)}) conditional(s32[]{:T(128)} %convert_element_type.336, () %tuple.116, (s32[]{:T(128)}, bf16[4,32,2048]{2,1,0:T(8,128)(2,1)}, bf16[4,32,2048]{2,1,0:T(8,128)(2,1)}, bf16[1024,2048]{1,0:T(8,128)(2,1)}, s32[4,32]{1,0:T(4,128)}, ...), branch_computations={%region_16.16_spmd, %region_17.25_spmd} | conditional | flops 2205094656 | bytes 49832296 | solution.py:193
  837.1 2.1 fusion.47
  841.5 4.6 fusion.71
  851.8 3.7 convolution_convert_fusion.5
  856.7 1.5 fusion.54
  860.8 2.0 fusion.62
  866.9 1.8 fusion.49
  872.0 2.9 fusion.139
  876.8 2.6 fusion.78
  884.3 47.8 %all-gather.3 = f32[65536]{0:T(1024)S(1)} all-gather(f32[2048]{0:T(1024)} %get-tuple-element.237), channel_id=5, replica_groups=mesh['section'=8,'dp'=32] {'dp'}, dimensions={0}, use_global_device_ids=true | all-gather | bytes 270336 | tf_op jit(solution)/shard_map/all_gather | solution.py:14
  (255 shorter events, 114.2 us)
Async XLA Ops:
  7.2 90.8 %all-gather.10.cloned.1.call-start = ((), (), s32[]{:S(2)}) async-start(), calls=%async_computation.2 | async-start | bytes 4325376 | tf_op jit(solution)/shard_map/all_gather | solution.py:130
  7.9 171.2 %all-gather.12.cloned.1.call-start = ((), (), s32[]{:S(2)}) async-start(), calls=%async_computation.3 | async-start | bytes 4325376 | tf_op jit(solution)/shard_map/all_gather | solution.py:132
  8.6 248.0 %all-gather.8.cloned.1.call-start = ((), (), s32[]{:S(2)}) async-start(), calls=%async_computation.1 | async-start | bytes 2162688 | tf_op jit(solution)/shard_map/all_gather | solution.py:131
  21.3 41.6 %all-to-all-start = ((bf16[32,4,2,2048]{3,2,1,0:T(2,128)(2,1)}), bf16[32,4,2,2048]{3,2,1,0:T(2,128)(2,1)S(1)}, u32[]{:S(2)}, u32[]{:S(2)}) async-start(bf16[32,4,2,2048]{3,2,1,0:T(2,128)(2,1)} %pad_maximum_fusion.3), calls=%async_computation | async-start | bytes 2097152 | tf_op jit(solution)/shard_map/all_to_all | solution.py:149
  276.6 2.8 collective-permute-start
  281.5 22.1 %collective-permute-start = (bf16[4,32,2048]{2,1,0:T(8,128)(2,1)S(1)}, bf16[4,32,2048]{2,1,0:T(8,128)(2,1)S(1)}, u32[]{:S(2)}, u32[]{:S(2)}) collective-permute-start(bf16[4,32,2048]{2,1,0:T(8,128)(2,1)S(1)} %get-tuple-element.784), channel_id=1, source_target_pairs={{0,32},{32,64},{64,96},{96,128},{128,160},{160,192},{192,224},{1,3... | collective-permute-start | bytes 1572872 | tf_op jit(solution)/shard_map/while/body/eval_jaxpr/ppermute | solution.py:175
  305.7 8.0 collective-permute-start
  315.8 28.4 %collective-permute-start = (bf16[4,32,2048]{2,1,0:T(8,128)(2,1)S(1)}, bf16[4,32,2048]{2,1,0:T(8,128)(2,1)S(1)}, u32[]{:S(2)}, u32[]{:S(2)}) collective-permute-start(bf16[4,32,2048]{2,1,0:T(8,128)(2,1)S(1)} %get-tuple-element.784), channel_id=1, source_target_pairs={{0,32},{32,64},{64,96},{96,128},{128,160},{160,192},{192,224},{1,3... | collective-permute-start | bytes 1572872 | tf_op jit(solution)/shard_map/while/body/eval_jaxpr/ppermute | solution.py:175
  346.2 10.5 %collective-permute-start = (bf16[4,32,2048]{2,1,0:T(8,128)(2,1)S(1)}, bf16[4,32,2048]{2,1,0:T(8,128)(2,1)S(1)}, u32[]{:S(2)}, u32[]{:S(2)}) collective-permute-start(bf16[4,32,2048]{2,1,0:T(8,128)(2,1)S(1)} %get-tuple-element.784), channel_id=1, source_target_pairs={{0,32},{32,64},{64,96},{96,128},{128,160},{160,192},{192,224},{1,3... | collective-permute-start | bytes 1572872 | tf_op jit(solution)/shard_map/while/body/eval_jaxpr/ppermute | solution.py:175
  358.7 15.0 %collective-permute-start = (bf16[4,32,2048]{2,1,0:T(8,128)(2,1)S(1)}, bf16[4,32,2048]{2,1,0:T(8,128)(2,1)S(1)}, u32[]{:S(2)}, u32[]{:S(2)}) collective-permute-start(bf16[4,32,2048]{2,1,0:T(8,128)(2,1)S(1)} %get-tuple-element.784), channel_id=1, source_target_pairs={{0,32},{32,64},{64,96},{96,128},{128,160},{160,192},{192,224},{1,3... | collective-permute-start | bytes 1572872 | tf_op jit(solution)/shard_map/while/body/eval_jaxpr/ppermute | solution.py:175
  375.8 10.5 %collective-permute-start = (bf16[4,32,2048]{2,1,0:T(8,128)(2,1)S(1)}, bf16[4,32,2048]{2,1,0:T(8,128)(2,1)S(1)}, u32[]{:S(2)}, u32[]{:S(2)}) collective-permute-start(bf16[4,32,2048]{2,1,0:T(8,128)(2,1)S(1)} %get-tuple-element.784), channel_id=1, source_target_pairs={{0,32},{32,64},{64,96},{96,128},{128,160},{160,192},{192,224},{1,3... | collective-permute-start | bytes 1572872 | tf_op jit(solution)/shard_map/while/body/eval_jaxpr/ppermute | solution.py:175
  388.3 25.9 %collective-permute-start = (bf16[4,32,2048]{2,1,0:T(8,128)(2,1)S(1)}, bf16[4,32,2048]{2,1,0:T(8,128)(2,1)S(1)}, u32[]{:S(2)}, u32[]{:S(2)}) collective-permute-start(bf16[4,32,2048]{2,1,0:T(8,128)(2,1)S(1)} %get-tuple-element.784), channel_id=1, source_target_pairs={{0,32},{32,64},{64,96},{96,128},{128,160},{160,192},{192,224},{1,3... | collective-permute-start | bytes 1572872 | tf_op jit(solution)/shard_map/while/body/eval_jaxpr/ppermute | solution.py:175
  418.7 10.2 %collective-permute-start.1 = (bf16[4,32,2048]{2,1,0:T(8,128)(2,1)}, bf16[4,32,2048]{2,1,0:T(8,128)(2,1)S(1)}, u32[]{:S(2)}, u32[]{:S(2)}) collective-permute-start(bf16[4,32,2048]{2,1,0:T(8,128)(2,1)} %get-tuple-element.682), channel_id=1, source_target_pairs={{32,0},{64,32},{96,64},{128,96},{160,128},{192,160},{224,192},{33,... | collective-permute-start | bytes 1572872 | tf_op jit(solution)/shard_map/while/body/eval_jaxpr/ppermute | solution.py:196
  428.8 0.9 copy-start.1
  433.2 15.9 %collective-permute-start.1 = (bf16[4,32,2048]{2,1,0:T(8,128)(2,1)}, bf16[4,32,2048]{2,1,0:T(8,128)(2,1)S(1)}, u32[]{:S(2)}, u32[]{:S(2)}) collective-permute-start(bf16[4,32,2048]{2,1,0:T(8,128)(2,1)} %get-tuple-element.682), channel_id=1, source_target_pairs={{32,0},{64,32},{96,64},{128,96},{160,128},{192,160},{224,192},{33,... | collective-permute-start | bytes 1572872 | tf_op jit(solution)/shard_map/while/body/eval_jaxpr/ppermute | solution.py:196
  449.2 0.9 copy-start.1
  453.6 10.7 %collective-permute-start.1 = (bf16[4,32,2048]{2,1,0:T(8,128)(2,1)}, bf16[4,32,2048]{2,1,0:T(8,128)(2,1)S(1)}, u32[]{:S(2)}, u32[]{:S(2)}) collective-permute-start(bf16[4,32,2048]{2,1,0:T(8,128)(2,1)} %get-tuple-element.682), channel_id=1, source_target_pairs={{32,0},{64,32},{96,64},{128,96},{160,128},{192,160},{224,192},{33,... | collective-permute-start | bytes 1572872 | tf_op jit(solution)/shard_map/while/body/eval_jaxpr/ppermute | solution.py:196
  464.2 0.9 copy-start.1
  468.6 26.3 %collective-permute-start.1 = (bf16[4,32,2048]{2,1,0:T(8,128)(2,1)}, bf16[4,32,2048]{2,1,0:T(8,128)(2,1)S(1)}, u32[]{:S(2)}, u32[]{:S(2)}) collective-permute-start(bf16[4,32,2048]{2,1,0:T(8,128)(2,1)} %get-tuple-element.682), channel_id=1, source_target_pairs={{32,0},{64,32},{96,64},{128,96},{160,128},{192,160},{224,192},{33,... | collective-permute-start | bytes 1572872 | tf_op jit(solution)/shard_map/while/body/eval_jaxpr/ppermute | solution.py:196
  495.0 0.9 copy-start.1
  499.3 10.7 %collective-permute-start.1 = (bf16[4,32,2048]{2,1,0:T(8,128)(2,1)}, bf16[4,32,2048]{2,1,0:T(8,128)(2,1)S(1)}, u32[]{:S(2)}, u32[]{:S(2)}) collective-permute-start(bf16[4,32,2048]{2,1,0:T(8,128)(2,1)} %get-tuple-element.682), channel_id=1, source_target_pairs={{32,0},{64,32},{96,64},{128,96},{160,128},{192,160},{224,192},{33,... | collective-permute-start | bytes 1572872 | tf_op jit(solution)/shard_map/while/body/eval_jaxpr/ppermute | solution.py:196
  510.0 0.9 copy-start.1
  514.4 15.4 %collective-permute-start.1 = (bf16[4,32,2048]{2,1,0:T(8,128)(2,1)}, bf16[4,32,2048]{2,1,0:T(8,128)(2,1)S(1)}, u32[]{:S(2)}, u32[]{:S(2)}) collective-permute-start(bf16[4,32,2048]{2,1,0:T(8,128)(2,1)} %get-tuple-element.682), channel_id=1, source_target_pairs={{32,0},{64,32},{96,64},{128,96},{160,128},{192,160},{224,192},{33,... | collective-permute-start | bytes 1572872 | tf_op jit(solution)/shard_map/while/body/eval_jaxpr/ppermute | solution.py:196
  529.9 0.9 copy-start.1
  534.2 298.5 %collective-permute-start.1 = (bf16[4,32,2048]{2,1,0:T(8,128)(2,1)}, bf16[4,32,2048]{2,1,0:T(8,128)(2,1)S(1)}, u32[]{:S(2)}, u32[]{:S(2)}) collective-permute-start(bf16[4,32,2048]{2,1,0:T(8,128)(2,1)} %get-tuple-element.682), channel_id=1, source_target_pairs={{32,0},{64,32},{96,64},{128,96},{160,128},{192,160},{224,192},{33,... | collective-permute-start | bytes 1572872 | tf_op jit(solution)/shard_map/while/body/eval_jaxpr/ppermute | solution.py:196
  832.8 0.9 copy-start.1
  836.6 4.8 copy-start.20
  839.3 0.7 copy-start.13
  841.4 6.6 copy-start.2
  841.4 6.6 copy-start.4
  849.1 1.6 copy-start.8
  856.7 2.4 copy-start.11
  856.7 4.0 copy-start.9
  860.7 3.0 copy-start.10
  860.7 3.0 copy-start.12
  860.8 3.0 copy-start.18
  862.8 1.9 copy-start.7
  862.8 1.8 copy-start.14
  863.7 1.2 copy-start.15
  863.7 3.2 copy-start.3
  863.7 3.1 copy-start.5
  863.7 3.1 copy-start.19
  869.1 5.8 copy-start
  869.1 5.8 copy-start.6
  872.0 4.8 copy-start.17
  872.0 4.8 copy-start.21
  879.4 4.0 collective-permute-start.1
  883.4 0.9 copy-start.1
  (1 other events, 0.5 us)
Sparse Core Ops, SparseCore 0:
  10.6 87.3 all-gather.9
  100.5 78.5 all-gather.11
  181.7 74.8 all-gather.7
